TPU v7x, 32 devices: a whole 2x2x4 slice. The times are simulated.
32 devices in a mesh: grp: 4 (over z), mem: 8 (over y, x, core).
Axes of the slice: x: 2, y: 2, z: 4, core: 2. Of those that a mesh axis runs over, the one named last changes fastest.
Arguments:
- design: bfloat16 [8192, 1024], P(('grp', 'mem'))
- active_blocks: int32 [32, 8], P(('grp', 'mem')), may hold values from 0 to 31, as said below
- ridge: float32 [4096], replicated, may hold values from 0.5 to 2
Outputs:
- factored: float32 [8, 128, 128, 128], P('mem', 'grp')
Inputs may be any that keep to these rules, and one draw needn't show every extreme that they name: active_blocks[d, a] % 8 == a for every device d and position a, so a device's blocks are distinct.
All inputs are finite; a program needn't handle non-finite values.
Results may differ from a plain program's by a relative error of at most 0.0003.
Values sent between devices are 32-bit elements; how exact they have to be, the bound alone decides.
No kernel may reach another device: no remote copies, remote signals or barrier semaphores. Data moves between devices by JAX's collectives and lax.ppermute only.
A program may use at most 64 MiB of HBM per device.

v0:
```python
import jax
import jax.numpy as jnp
from jax import lax
from jax.sharding import PartitionSpec as P

NB = 32
BLK = 128
ACT = 8
HI = lax.Precision.HIGHEST


def panel_solve(column):
    count = column.shape[0]
    chol = jnp.linalg.cholesky(column[0])
    stacked = jnp.transpose(column, (2, 0, 1)).reshape(BLK, count * BLK)
    solved = lax.linalg.triangular_solve(chol, stacked, left_side=True, lower=True)
    lower_col = jnp.transpose(solved.reshape(BLK, count, BLK), (1, 2, 0))
    return lower_col.at[0].set(chol)


def apply_step(tiles, lower_col, step, tile_rows, tile_cols):
    left_tiles = jnp.take(lower_col, jnp.maximum(tile_rows - step, 0), axis=0)
    right_tiles = jnp.take(lower_col, jnp.maximum(tile_cols - step, 0), axis=0)
    update = jnp.einsum("tpr,tqr->tpq", left_tiles, right_tiles, precision=HI)
    trailing = ((tile_rows > step) & (tile_cols > step))[:, None, None]
    on_column = ((tile_cols == step) & (tile_rows >= step))[:, None, None]
    on_row = ((tile_rows == step) & (tile_cols > step))[:, None, None]
    tiles = jnp.where(trailing, tiles - update, tiles)
    tiles = jnp.where(on_column, left_tiles, tiles)
    tiles = jnp.where(on_row, jnp.transpose(right_tiles, (0, 2, 1)), tiles)
    return tiles


def column_picker(step, tile_rows, tile_cols):
    wanted = step + jnp.arange(NB - step, dtype=jnp.int32)
    inside = (tile_cols == step) & (tile_rows >= step)
    return ((tile_rows[None, :] == wanted[:, None]) & inside[None, :]).astype(jnp.float32)


def on_device_general(design, active_blocks, ridge):
    n_mem = lax.axis_size("mem")
    n_grp = lax.axis_size("grp")
    member = lax.axis_index("mem")
    group = lax.axis_index("grp")
    classes = n_mem // 8
    per_pos = ACT // classes
    per_row = NB // ACT
    slot_count = NB // classes * per_row
    owned_count = slot_count // n_grp
    row_count = design.shape[0]
    residue = member // 8
    position = member % 8
    everyone = lax.all_gather(active_blocks, "mem", axis=0, tiled=True)
    blocks = design.reshape(row_count, ACT, BLK)
    left = blocks.reshape(row_count, per_pos, classes, BLK)
    outgoing = jnp.einsum("ncqk,nbl->qbckl", left, blocks, preferred_element_type=jnp.float32)
    outgoing = outgoing.reshape(n_mem, per_pos, BLK, BLK)
    received = lax.all_to_all(outgoing, "mem", split_axis=0, concat_axis=0, tiled=True)
    row_ids = jnp.take(everyone.reshape(n_mem, per_pos, classes), residue, axis=2)
    col_ids = jnp.take(everyone, position, axis=1)
    targets = row_ids // classes * per_row + (col_ids // 8)[:, None]
    onehot = (
        targets.reshape(-1)[None, :] == jnp.arange(slot_count, dtype=jnp.int32)[:, None]
    ).astype(jnp.float32)
    sums = jnp.dot(
        onehot,
        received.reshape(n_mem * per_pos, BLK * BLK),
        precision=HI,
        preferred_element_type=jnp.float32,
    )
    sums = sums.reshape(slot_count, BLK, BLK)
    owned = lax.psum_scatter(sums, "grp", scatter_dimension=0, tiled=True)
    slots = group * owned_count + jnp.arange(owned_count, dtype=jnp.int32)
    tile_rows = slots // per_row * classes + residue
    tile_cols = slots % per_row * 8 + position
    ridge_blocks = jnp.take(ridge.reshape(NB, BLK), tile_rows, axis=0)
    same = (tile_rows == tile_cols).astype(jnp.float32)
    extra = jnp.eye(BLK, dtype=jnp.float32)[None] * ridge_blocks[:, None, :] * same[:, None, None]
    divisor = jnp.float32(row_count * n_grp * n_mem // 16)
    tiles = owned / divisor + extra
    picker = column_picker(0, tile_rows, tile_cols)
    partial_value = jnp.einsum("it,tpq->ipq", picker, tiles, precision=HI)
    column = lax.psum(partial_value, ("grp", "mem"))
    lower_col = panel_solve(column)
    tiles = apply_step(tiles, lower_col, 0, tile_rows, tile_cols)
    return tiles[None]


def on_device_fast(design, active_blocks, ridge):
    n_mem = lax.axis_size("mem")
    n_grp = lax.axis_size("grp")
    member = lax.axis_index("mem")
    group = lax.axis_index("grp")
    per_row = NB // ACT
    row_count = design.shape[0]
    divisor = jnp.float32(row_count * n_grp * n_mem // 16)
    eye = jnp.eye(BLK, dtype=jnp.float32)
    ridge_blocks = ridge.reshape(NB, BLK)
    everyone = lax.all_gather(active_blocks, "mem", axis=0, tiled=True)
    blocks = design.reshape(row_count, ACT, BLK)
    outgoing = jnp.einsum("nak,nbl->bakl", blocks, blocks, preferred_element_type=jnp.float32)
    mine00 = jnp.where(active_blocks[0, 0] == 0, outgoing[0, 0], 0.0)
    gram00 = lax.psum(mine00, ("grp", "mem"))
    a00 = gram00 / divisor + eye * ridge_blocks[0][None, :]
    chol = jnp.linalg.cholesky(a00)
    chol_inv = lax.linalg.triangular_solve(chol, eye, left_side=True, lower=True)
    received = lax.all_to_all(outgoing, "mem", split_axis=0, concat_axis=0, tiled=True)
    received = received.reshape(n_mem, ACT, BLK, BLK)
    row_grp = everyone // 8
    col_grp = jnp.take(everyone, member, axis=1) // 8
    grp_ids = jnp.arange(n_grp, dtype=jnp.int32)
    q_ids = jnp.arange(per_row, dtype=jnp.int32)
    mask = (
        (row_grp[:, :, None, None] == grp_ids[None, None, :, None])
        & (col_grp[:, None, None, None] == q_ids[None, None, None, :])
    ).astype(jnp.float32)
    main = jnp.einsum("sagq,sakl->gaqkl", mask, received, precision=HI)
    main = main.reshape(n_grp, ACT * per_row, BLK, BLK)
    col_mask = ((col_grp[:, None] == grp_ids[None, :]) & (everyone[:, 0:1] == 0)).astype(
        jnp.float32
    )
    col_part = jnp.einsum("sg,slk->gkl", col_mask, received[:, 0], precision=HI)
    send = jnp.concatenate([main, col_part[:, None]], axis=1)
    send = send.reshape(n_grp * (ACT * per_row + 1), BLK, BLK)
    got = lax.psum_scatter(send, "grp", scatter_dimension=0, tiled=True)
    owned = got[: ACT * per_row]
    col_tile = got[ACT * per_row] / divisor
    t = jnp.arange(ACT * per_row, dtype=jnp.int32)
    tile_rows = group * 8 + t // per_row
    tile_cols = t % per_row * 8 + member
    same = (tile_rows == tile_cols).astype(jnp.float32)
    diag = eye[None] * jnp.take(ridge_blocks, tile_rows, axis=0)[:, None, :] * same[:, None, None]
    tiles = owned / divisor + diag
    col_rows = lax.all_gather(col_tile, "mem", axis=0, tiled=False)
    col_cols = lax.all_gather(col_tile, "grp", axis=0, tiled=False)
    p_rows = jnp.einsum("ipr,qr->ipq", col_rows, chol_inv, precision=HI)
    p_cols = jnp.einsum("ipr,qr->ipq", col_cols, chol_inv, precision=HI)
    row_ids = group * 8 + jnp.arange(8, dtype=jnp.int32)
    col_ids = jnp.arange(per_row, dtype=jnp.int32) * 8 + member
    p_rows = jnp.where((row_ids == 0)[:, None, None], chol[None], p_rows)
    p_cols = jnp.where((col_ids == 0)[:, None, None], chol[None], p_cols)
    update = jnp.einsum("apr,qsr->aqps", p_rows, p_cols, precision=HI)
    update = update.reshape(ACT * per_row, BLK, BLK)
    left_tiles = jnp.repeat(p_rows, per_row, axis=0)
    right_tiles = jnp.tile(p_cols, (ACT, 1, 1))
    trailing = ((tile_rows > 0) & (tile_cols > 0))[:, None, None]
    on_column = (tile_cols == 0)[:, None, None]
    on_row = ((tile_rows == 0) & (tile_cols > 0))[:, None, None]
    tiles = jnp.where(trailing, tiles - update, tiles)
    tiles = jnp.where(on_column, left_tiles, tiles)
    tiles = jnp.where(on_row, jnp.transpose(right_tiles, (0, 2, 1)), tiles)
    return tiles[None]


def solution(mesh):
    n_mem = mesh.shape["mem"]
    n_grp = mesh.shape["grp"]
    fast = n_mem == 8 and n_grp * 8 == NB
    body = on_device_fast if fast else on_device_general
    in_specs = (P(("grp", "mem"), None), P(("grp", "mem"), None), P())
    out_specs = P("mem", "grp", None, None)
    return jax.shard_map(body, mesh=mesh, in_specs=in_specs, out_specs=out_specs, check_vma=False)
```

profile of v0, /device:TPU:0, one launch (start us, length us, event | category | flops | bytes accessed | tf_op | source)
XLA Modules:
  0.0 329.3 jit_solution(12028579138386191531)
XLA Ops:
  7.4 1.1 copy.56
  8.5 3.8 %convolution_bitcast_fusion.1 = f32[8,8,128,128]{3,2,1,0:T(8,128)} fusion(bf16[256,8,128,1]{2,1,0,3:T(8,128)(2,1)S(1)} %bitcast.82, bf16[256,1024]{1,0:T(8,128)(2,1)} %param.3), kind=kOutput, calls=%fused_computation.5 | convolution fusion | flops 536870912 | bytes 5242880 | tf_op jit(solution)/shard_map/nak,nbl->bakl/dot_general | solution.py:101
  12.3 5.3 %all-to-all-start = ((f32[8,8,128,128]{3,2,1,0:T(8,128)}), f32[8,8,128,128]{3,2,1,0:T(8,128)}, u32[]{:S(2)}, u32[]{:S(2)}) async-start(f32[8,8,128,128]{3,2,1,0:T(8,128)} %convolution_bitcast_fusion.1), calls=%async_computation | async-start | bytes 8388608 | tf_op jit(solution)/shard_map/all_to_all | solution.py:107
  17.7 1.5 fusion.10
  19.2 50.7 %all-gather = s32[8,1,8]{2,1,0:T(1,128)S(1)} all-gather(s32[1,1,8]{2,1,0:T(1,128)S(1)} %bitcast.87), channel_id=1, replica_groups=mesh['grp'=4,'mem'=8] {'mem'}, dimensions={0}, use_global_device_ids=true | all-gather | bytes 288 | tf_op jit(solution)/shard_map/all_gather | solution.py:99
  70.0 0.3 fusion.19
  70.3 0.1 fusion.21
  70.5 1.1 slice_bitcast_fusion
  71.6 0.7 convolution_bitcast_fusion.3
  72.2 0.1 copy.43
  72.4 14.0 %convolution_bitcast_fusion = f32[4,8,4,128,128]{4,2,0,3,1:T(4,128)S(1)} fusion(f32[8,8,128,128,1]{3,2,1,0,4:T(8,128)} %bitcast.6, pred[8,4]{0,1:T(4,128)(4,1)S(1)} %iota_compare_fusion.4, pred[8,8,4]{0,2,1:T(4,128)(4,1)S(1)} %iota_compare_fusion.3), kind=kOutput, calls=%fused_computation.2 | convolution fusion | flops 201327616 | bytes 12583200 | tf_op jit(solution)/shard_map/sagq,sakl->gaqkl/dot_general | solution.py:117
  86.4 2.7 copy.41
  89.1 3.9 %pad_maximum_fusion = f32[4,33,128,128]{3,2,1,0:T(8,128)} fusion(f32[4,1,128,128]{3,2,1,0:T(8,128)S(1)} %copy.43, f32[4,32,128,128]{3,2,1,0:T(8,128)S(1)} %bitcast.80), kind=kLoop, calls=%fused_computation.1 | loop fusion | flops 2162688 | bytes 17301504 | tf_op jit(solution)/shard_map/concatenate | solution.py:123
  93.1 0.7 copy-done
  93.8 0.6 gather_fusion
  94.5 167.3 %all-reduce.2.cloned.1.call-done = f32[128,128]{1,0:T(8,128)} async-done(((f32[128,128]{1,0:T(8,128)}), f32[128,128]{1,0:T(8,128)}) %all-reduce.2.cloned.1.call-update) | async-done | bytes 65552 | tf_op jit(solution)/shard_map/psum | solution.py:103
  261.8 0.9 select_add_fusion
  262.8 0.9 fusion.12
  263.7 11.7 %cholesky.23 = f32[128,128]{1,0:T(8,128)S(1)} custom-call(f32[128,128]{1,0:T(8,128)S(1)} %fusion.12), custom_call_target="Cholesky" | custom-call | tf_op jit(solution)/shard_map/jit(cholesky)/cholesky | solution.py:105
  275.4 0.6 compare_reduce_fusion
  276.1 0.7 select_bitcast_fusion
  276.7 9.8 %custom-call.6 = f32[1,128,128]{1,2,0:T(8,128)S(1)} custom-call(f32[1,128,128]{2,1,0:T(8,128)S(1)} %get-tuple-element.16), custom_call_target="InvertDiagBlocksLowerTriangular" | custom-call | tf_op jit(solution)/shard_map/triangular_solve | solution.py:106
  286.5 0.2 convolution_bitcast_fusion.4
  286.8 0.8 slice_multiply_fusion.1
  287.7 15.1 %all_gather.12 = f32[4,128,128]{2,1,0:T(8,128)S(1)} all-gather(f32[1,128,128]{2,1,0:T(8,128)S(1)} %slice_multiply_fusion.1), channel_id=1, replica_groups=mesh['grp'=4,'mem'=8] {'grp'}, dimensions={0}, use_global_device_ids=true | all-gather | bytes 327680 | tf_op jit(solution)/shard_map/all_gather | solution.py:135
  302.8 10.0 %all_gather.13 = f32[8,128,128]{2,1,0:T(8,128)S(1)} all-gather(f32[1,128,128]{2,1,0:T(8,128)S(1)} %slice_multiply_fusion.1), channel_id=1, replica_groups=mesh['grp'=4,'mem'=8] {'mem'}, dimensions={0}, use_global_device_ids=true | all-gather | bytes 589824 | tf_op jit(solution)/shard_map/all_gather | solution.py:134
  312.8 0.4 convolution_select_fusion.1
  313.2 0.1 copy.44
  313.3 0.6 convolution_select_fusion
  313.9 1.8 convolution_bitcast_fusion.2
  315.7 1.9 copy.45
  317.6 4.3 %fusion.3 = f32[1,32,128,128]{3,2,1,0:T(8,128)} fusion(f32[33,128,128]{2,1,0:T(8,128)} %reduce-scatter.2.cloned.1.call-done, f32[8,4,128,128]{3,2,1,0:T(8,128)} %copy.45, f32[32]{0:T(128)S(1)} %get-tuple-element.18, f32[32,128]{1,0:T(8,128)S(1)} %broadcast_select_fusion, f32[128,128]{1,0:T(8,128)S(1)} %fusion.13, ...), kind=kLoop, calls=%fused_computation.8 | loop fusion | flops 4194304 | bytes 7160032 | tf_op jit(solution)/shard_map/broadcast_in_dim | solution.py:152
  (26 shorter events, 0.5 us)
Async XLA Ops:
  12.3 5.3 %copy-start.1 = (s32[1,8]{1,0:T(1,128)S(1)}, s32[1,8]{1,0:T(1,128)}, u32[]{:S(2)}) copy-start(s32[1,8]{1,0:T(1,128)} %param.4) | copy-start | bytes 100
  12.3 58.2 %all-to-all-start = ((f32[8,8,128,128]{3,2,1,0:T(8,128)}), f32[8,8,128,128]{3,2,1,0:T(8,128)}, u32[]{:S(2)}, u32[]{:S(2)}) async-start(f32[8,8,128,128]{3,2,1,0:T(8,128)} %convolution_bitcast_fusion.1), calls=%async_computation | async-start | bytes 8388608 | tf_op jit(solution)/shard_map/all_to_all | solution.py:107
  17.6 244.3 %all-reduce.2.cloned.1.call-start = ((), (), s32[]{:S(2)}) async-start(), calls=%async_computation.2 | async-start | bytes 131072 | tf_op jit(solution)/shard_map/psum | solution.py:103
  19.2 267.6 %reduce-scatter.2.cloned.1.call-start = ((), (), s32[]{:S(2)}) async-start(), calls=%async_computation.3 | async-start | bytes 10813440 | tf_op jit(solution)/shard_map/reduce_scatter | solution.py:125
  93.0 0.7 copy-start
Sparse Core Ops, SparseCore 0:
  24.0 237.8 all-reduce.1
Sparse Core Ops, SparseCore 1:
  93.1 149.5 reduce-scatter.1
where the time goes:
time: 330 us; the launch traced here: 329 us
  waiting for transfers between devices  167 us (51%)
  blocking collectives  75.8 us (23%)
  other arithmetic  35.7 us (11%)
  matrix products  21.5 us (7%)
  between operations  15.1 us (5%)
  local copies, waits for them, and re-layouts  8.48 us (3%)
  starting transfers between devices  5.37 us (2%)
    psum x1, waiting for transfers between devices, on_device_fast(): gram00 = lax.psum(mine00, ('grp', 'mem'))  167 us
    all_gather x1, blocking collectives, on_device_fast(): everyone = lax.all_gather(active_blocks, 'mem', axis=0, tiled=True)  50.7 us
    all_gather x1, blocking collectives, on_device_fast(): col_cols = lax.all_gather(col_tile, 'grp', axis=0, tiled=False)  15.1 us
    dot_general x1, matrix products, on_device_fast(): main = jnp.einsum('sagq,sakl->gaqkl', mask, received, precision=HI)  14 us
    another operation x3, other arithmetic, on_device_fast(): chol = jnp.linalg.cholesky(a00)  12.4 us
    another operation x2, other arithmetic, on_device_fast(): lax.linalg.triangular_solve(chol, eye, left_side=True, lower=True)  10.5 us
    all_gather x1, blocking collectives, on_device_fast(): col_rows = lax.all_gather(col_tile, 'mem', axis=0, tiled=False)  10 us
  transfers between devices with their start and end apart: 3, of which 1 were waited for; matrix products, arithmetic and copies ran while one was open for 15% of the time, Pallas kernels for 0%

commit v1 on v0

--- a/solution.py
+++ b/solution.py
@@ -100,7 +100,7 @@
     blocks = design.reshape(row_count, ACT, BLK)
     outgoing = jnp.einsum("nak,nbl->bakl", blocks, blocks, preferred_element_type=jnp.float32)
     mine00 = jnp.where(active_blocks[0, 0] == 0, outgoing[0, 0], 0.0)
-    gram00 = lax.psum(mine00, ("grp", "mem"))
+    gram00 = lax.psum(lax.psum(mine00, "mem"), "grp")
     a00 = gram00 / divisor + eye * ridge_blocks[0][None, :]
     chol = jnp.linalg.cholesky(a00)
     chol_inv = lax.linalg.triangular_solve(chol, eye, left_side=True, lower=True)

time: 330 us -> 314 us (0.952)
  waiting for transfers between devices: 167 us -> 153 us
    psum x1 -> x2, waiting for transfers between devices: 167 us -> 27.6 us  [on_device_fast(): gram00 = lax.psum(lax.psum(mine00, 'mem'), 'grp')]
    reduce_scatter x1, waiting for transfers between devices: 0.03 us -> 126 us  [on_device_fast(): got = lax.psum_scatter(send, 'grp', scatter_dimension=0, tiled=True)]
  transfers between devices with their start and end apart: 3 -> 4, of which waited for: 1 -> 3; matrix products, arithmetic and copies ran while one was open for 15% -> 16% of each run, Pallas kernels for 0% -> 0%
where the time goes in v1:
time: 314 us
  waiting for transfers between devices  153 us (49%)
  blocking collectives  75.8 us (24%)
  other arithmetic  35.7 us (11%)
  matrix products  21.4 us (7%)
  between operations  13.3 us (4%)
  local copies, waits for them, and re-layouts  8.48 us (3%)
  starting transfers between devices  5.41 us (2%)
    reduce_scatter x1, waiting for transfers between devices, on_device_fast(): got = lax.psum_scatter(send, 'grp', scatter_dimension=0, tiled=True)  126 us
    all_gather x1, blocking collectives, on_device_fast(): everyone = lax.all_gather(active_blocks, 'mem', axis=0, tiled=True)  51 us
    psum x2, waiting for transfers between devices, on_device_fast(): gram00 = lax.psum(lax.psum(mine00, 'mem'), 'grp')  27.6 us
    all_gather x1, blocking collectives, on_device_fast(): col_cols = lax.all_gather(col_tile, 'grp', axis=0, tiled=False)  14.7 us
    dot_general x1, matrix products, on_device_fast(): main = jnp.einsum('sagq,sakl->gaqkl', mask, received, precision=HI)  14 us
    another operation x3, other arithmetic, on_device_fast(): chol = jnp.linalg.cholesky(a00)  12.4 us
    another operation x2, other arithmetic, on_device_fast(): lax.linalg.triangular_solve(chol, eye, left_side=True, lower=True)  10.5 us
    all_gather x1, blocking collectives, on_device_fast(): col_rows = lax.all_gather(col_tile, 'mem', axis=0, tiled=False)  10.1 us
  transfers between devices with their start and end apart: 4, of which 3 were waited for; matrix products, arithmetic and copies ran while one was open for 16% of the time, Pallas kernels for 0%

profile of v1, /device:TPU:0, one launch (start us, length us, event | category | flops | bytes accessed | tf_op | source)
XLA Modules:
  0.0 313.6 jit_solution(16948941735167242482)
XLA Ops:
  6.5 1.1 copy.56
  7.7 3.8 %convolution_bitcast_fusion.1 = f32[8,8,128,128]{3,2,1,0:T(8,128)} fusion(bf16[256,8,128,1]{2,1,0,3:T(8,128)(2,1)S(1)} %bitcast.82, bf16[256,1024]{1,0:T(8,128)(2,1)} %param.3), kind=kOutput, calls=%fused_computation.5 | convolution fusion | flops 536870912 | bytes 5242880 | tf_op jit(solution)/shard_map/nak,nbl->bakl/dot_general | solution.py:101
  11.4 5.3 %all-to-all-start = ((f32[8,8,128,128]{3,2,1,0:T(8,128)}), f32[8,8,128,128]{3,2,1,0:T(8,128)}, u32[]{:S(2)}, u32[]{:S(2)}) async-start(f32[8,8,128,128]{3,2,1,0:T(8,128)} %convolution_bitcast_fusion.1), calls=%async_computation | async-start | bytes 8388608 | tf_op jit(solution)/shard_map/all_to_all | solution.py:107
  16.8 1.5 fusion.10
  18.4 51.0 %all-gather = s32[8,1,8]{2,1,0:T(1,128)S(1)} all-gather(s32[1,1,8]{2,1,0:T(1,128)S(1)} %bitcast.87), channel_id=1, replica_groups=mesh['grp'=4,'mem'=8] {'mem'}, dimensions={0}, use_global_device_ids=true | all-gather | bytes 288 | tf_op jit(solution)/shard_map/all_gather | solution.py:99
  69.5 0.3 fusion.19
  69.9 15.8 %all-reduce.3.cloned.1.call-done = f32[128,128]{1,0:T(8,128)} async-done(((f32[128,128]{1,0:T(8,128)}), f32[128,128]{1,0:T(8,128)}) %all-reduce.3.cloned.1.call-update) | async-done | bytes 65552 | tf_op jit(solution)/shard_map/psum | solution.py:103
  85.9 1.1 slice_bitcast_fusion
  86.9 0.7 convolution_bitcast_fusion.3
  87.6 0.1 copy.43
  87.7 14.0 %convolution_bitcast_fusion = f32[4,8,4,128,128]{4,2,0,3,1:T(4,128)S(1)} fusion(f32[8,8,128,128,1]{3,2,1,0,4:T(8,128)} %bitcast.6, pred[8,4]{0,1:T(4,128)(4,1)S(1)} %iota_compare_fusion.4, pred[8,8,4]{0,2,1:T(4,128)(4,1)S(1)} %iota_compare_fusion.3), kind=kOutput, calls=%fused_computation.2 | convolution fusion | flops 201327616 | bytes 12583200 | tf_op jit(solution)/shard_map/sagq,sakl->gaqkl/dot_general | solution.py:117
  101.8 2.7 copy.41
  104.5 3.9 %pad_maximum_fusion = f32[4,33,128,128]{3,2,1,0:T(8,128)} fusion(f32[4,1,128,128]{3,2,1,0:T(8,128)S(1)} %copy.43, f32[4,32,128,128]{3,2,1,0:T(8,128)S(1)} %bitcast.80), kind=kLoop, calls=%fused_computation.1 | loop fusion | flops 2162688 | bytes 17301504 | tf_op jit(solution)/shard_map/concatenate | solution.py:123
  108.4 0.7 copy-done
  109.1 0.6 gather_fusion
  109.9 11.7 %all-reduce.5.cloned.1.call-done = f32[128,128]{1,0:T(8,128)} async-done(((f32[128,128]{1,0:T(8,128)}), f32[128,128]{1,0:T(8,128)}) %all-reduce.5.cloned.1.call-update) | async-done | bytes 65552 | tf_op jit(solution)/shard_map/psum | solution.py:103
  121.6 0.9 select_add_fusion
  122.6 0.9 fusion.12
  123.4 11.7 %cholesky.23 = f32[128,128]{1,0:T(8,128)S(1)} custom-call(f32[128,128]{1,0:T(8,128)S(1)} %fusion.12), custom_call_target="Cholesky" | custom-call | tf_op jit(solution)/shard_map/jit(cholesky)/cholesky | solution.py:105
  135.2 0.6 compare_reduce_fusion
  135.8 0.7 select_bitcast_fusion
  136.5 9.8 %custom-call.6 = f32[1,128,128]{1,2,0:T(8,128)S(1)} custom-call(f32[1,128,128]{2,1,0:T(8,128)S(1)} %get-tuple-element.16), custom_call_target="InvertDiagBlocksLowerTriangular" | custom-call | tf_op jit(solution)/shard_map/triangular_solve | solution.py:106
  146.3 0.2 convolution_bitcast_fusion.4
  146.5 125.8 %reduce-scatter.2.cloned.1.call-done = f32[33,128,128]{2,1,0:T(8,128)} async-done(((f32[132,128,128]{2,1,0:T(8,128)}), f32[33,128,128]{2,1,0:T(8,128)}) %reduce-scatter.2.cloned.1.call-update) | async-done | bytes 2162704 | tf_op jit(solution)/shard_map/reduce_scatter | solution.py:125
  272.3 0.8 slice_multiply_fusion.1
  273.2 14.7 %all_gather.12 = f32[4,128,128]{2,1,0:T(8,128)S(1)} all-gather(f32[1,128,128]{2,1,0:T(8,128)S(1)} %slice_multiply_fusion.1), channel_id=1, replica_groups=mesh['grp'=4,'mem'=8] {'grp'}, dimensions={0}, use_global_device_ids=true | all-gather | bytes 327680 | tf_op jit(solution)/shard_map/all_gather | solution.py:135
  287.9 10.1 %all_gather.13 = f32[8,128,128]{2,1,0:T(8,128)S(1)} all-gather(f32[1,128,128]{2,1,0:T(8,128)S(1)} %slice_multiply_fusion.1), channel_id=1, replica_groups=mesh['grp'=4,'mem'=8] {'mem'}, dimensions={0}, use_global_device_ids=true | all-gather | bytes 589824 | tf_op jit(solution)/shard_map/all_gather | solution.py:134
  298.0 0.4 convolution_select_fusion.1
  298.5 0.6 convolution_select_fusion
  299.1 1.8 convolution_bitcast_fusion.2
  300.9 1.9 copy.45
  302.8 4.3 %fusion.3 = f32[1,32,128,128]{3,2,1,0:T(8,128)} fusion(f32[33,128,128]{2,1,0:T(8,128)} %reduce-scatter.2.cloned.1.call-done, f32[8,4,128,128]{3,2,1,0:T(8,128)} %copy.45, f32[32]{0:T(128)S(1)} %get-tuple-element.18, f32[32,128]{1,0:T(8,128)S(1)} %broadcast_select_fusion, f32[128,128]{1,0:T(8,128)S(1)} %fusion.13, ...), kind=kLoop, calls=%fused_computation.8 | loop fusion | flops 4194304 | bytes 7160032 | tf_op jit(solution)/shard_map/broadcast_in_dim | solution.py:152
  (29 shorter events, 0.8 us)
Async XLA Ops:
  11.4 5.3 %copy-start.1 = (s32[1,8]{1,0:T(1,128)S(1)}, s32[1,8]{1,0:T(1,128)}, u32[]{:S(2)}) copy-start(s32[1,8]{1,0:T(1,128)} %param.4) | copy-start | bytes 100
  11.4 74.4 %all-to-all-start = ((f32[8,8,128,128]{3,2,1,0:T(8,128)}), f32[8,8,128,128]{3,2,1,0:T(8,128)}, u32[]{:S(2)}, u32[]{:S(2)}) async-start(f32[8,8,128,128]{3,2,1,0:T(8,128)} %convolution_bitcast_fusion.1), calls=%async_computation | async-start | bytes 8388608 | tf_op jit(solution)/shard_map/all_to_all | solution.py:107
  16.7 69.0 %all-reduce.3.cloned.1.call-start = ((), (), s32[]{:S(2)}) async-start(), calls=%async_computation.2 | async-start | bytes 131072 | tf_op jit(solution)/shard_map/psum | solution.py:103
  18.3 103.3 %all-reduce.5.cloned.1.call-start = ((), (), s32[]{:S(2)}) async-start(), calls=%async_computation.3 | async-start | bytes 131072 | tf_op jit(solution)/shard_map/psum | solution.py:103
  85.8 186.5 %reduce-scatter.2.cloned.1.call-start = ((), (), s32[]{:S(2)}) async-start(), calls=%async_computation.4 | async-start | bytes 10813440 | tf_op jit(solution)/shard_map/reduce_scatter | solution.py:125
  108.4 0.7 copy-start
Sparse Core Ops, SparseCore 0:
  20.6 65.1 all-reduce.2
  88.2 33.3 all-reduce.4
  124.0 148.3 reduce-scatter.1
